TPU v7x, 32 devices: a whole 2x2x4 slice. The times are simulated.
32 devices in a mesh: gx: 4 (over z), gy: 8 (over y, x, core).
Axes of the slice: x: 2, y: 2, z: 4, core: 2. Of those that a mesh axis runs over, the one named last changes fastest.
Arguments:
- forcing: float32 [2, 16, 64, 1024], P(None, None, 'gx', 'gy'), may hold values from -6 to 6
- viscosity: float32 [16, 64, 1024], P(None, 'gx', 'gy'), may hold values from 0.05 to 0.5
- observed: float32 [2, 64, 1024], P(None, 'gx', 'gy'), may hold values from -6 to 6
- beta_tiles: float32 [4, 128], P('gx', 'gy'), may hold values from 1 to 30
- ice_mask: int32 [64, 1024], P('gx', 'gy'), may hold values 0 or 1
- tile_owner: int32 [64, 1024], P('gx', 'gy'), may hold values from 0 to 127
Outputs:
- velocity: float32 [2, 16, 64, 1024], P(None, None, 'gx', 'gy')
- adjoint: float32 [2, 16, 64, 1024], P(None, None, 'gx', 'gy')
- grad_tiles: float32 [4, 128], P('gx', 'gy')
All inputs are finite; a program needn't handle non-finite values. No bound on the sum of `ice_mask` on one device may be relied on, other than what follows from the above.
Results may differ from a plain program's by a relative error of at most 0.000025.
Values sent between devices are 32-bit elements; how exact they have to be, the bound alone decides.
No kernel may reach another device: no remote copies, remote signals or barrier semaphores. Data moves between devices by JAX's collectives and lax.ppermute only.
A program may use at most 64 MiB of HBM per device.

v0:
```python
import jax
import jax.numpy as jnp
from jax import lax
from jax.sharding import PartitionSpec as P

PASSES = 4
OMEGA = 0.8
VERTICAL = 16.0
HALO = 2 * PASSES - 1


def with_halo(cells, sides, width):
    for axis, dim in sides:
        count = lax.axis_size(axis)
        ends = count - 1
        head = lax.slice_in_dim(cells, 0, width, axis=dim)
        tail = lax.slice_in_dim(cells, cells.shape[dim] - width, cells.shape[dim], axis=dim)
        cells = jnp.concatenate(
            [
                lax.ppermute(tail, axis, [(i, (i + 1) % count) for i in range(ends)]),
                cells,
                lax.ppermute(head, axis, [((i + 1) % count, i) for i in range(ends)]),
            ],
            axis=dim,
        )
    return cells


def lateral_terms(visc_pad):
    centre_visc = visc_pad[:, 1:-1, 1:-1]
    west_face = 0.5 * (centre_visc + visc_pad[:, :-2, 1:-1])
    east_face = 0.5 * (centre_visc + visc_pad[:, 2:, 1:-1])
    south_face = 0.5 * (centre_visc + visc_pad[:, 1:-1, :-2])
    north_face = 0.5 * (centre_visc + visc_pad[:, 1:-1, 2:])
    return (west_face, east_face, south_face, north_face)


def weights_xy():
    along_x = jnp.array([4.0, 1.0], jnp.float32).reshape(2, 1, 1, 1)
    along_y = jnp.array([1.0, 4.0], jnp.float32).reshape(2, 1, 1, 1)
    return (along_x, along_y)


def prepare(visc_pad, beta_col, ice_cover):
    faces = lateral_terms(visc_pad)
    west_face, east_face, south_face, north_face = faces
    along_x, along_y = weights_xy()
    centre_visc = visc_pad[:, 1:-1, 1:-1]
    vertical = VERTICAL * 0.5 * (centre_visc[:-1] + centre_visc[1:])
    zero_row = jnp.zeros_like(centre_visc[:1])
    upper_link = jnp.concatenate([vertical, zero_row], 0)
    lower_link = jnp.concatenate([zero_row, vertical], 0)
    basal = jnp.concatenate([jnp.zeros_like(centre_visc[:-1]), beta_col[None]], 0)
    diagonal = along_x * (west_face + east_face) + along_y * (south_face + north_face)
    diagonal = diagonal + upper_link + lower_link + basal + (1.0 - ice_cover)
    layer_count = visc_pad.shape[0]
    ratio_list = []
    inverse_list = []
    for layer_idx in range(layer_count):
        pivot = diagonal[:, layer_idx]
        if layer_idx > 0:
            pivot = pivot + lower_link[layer_idx] * ratio_list[-1]
        inverse = 1.0 / pivot
        inverse_list.append(inverse)
        ratio_list.append(-upper_link[layer_idx] * inverse)
    return (faces, lower_link, jnp.stack(ratio_list, 1), jnp.stack(inverse_list, 1))


def relax(vel_pad, rhs_field, faces, lower_link, ratios, inverses, ice_cover):
    west_face, east_face, south_face, north_face = faces
    along_x, along_y = weights_xy()
    lateral = along_x * (west_face * vel_pad[:, :, :-2, 1:-1] + east_face * vel_pad[:, :, 2:, 1:-1])
    lateral = lateral + along_y * (
        south_face * vel_pad[:, :, 1:-1, :-2] + north_face * vel_pad[:, :, 1:-1, 2:]
    )
    right_side = rhs_field + lateral
    layer_count = right_side.shape[1]
    forward_list = []
    for layer_idx in range(layer_count):
        value = right_side[:, layer_idx]
        if layer_idx > 0:
            value = value + lower_link[layer_idx] * forward_list[-1]
        forward_list.append(value * inverses[:, layer_idx])
    solved = [None] * layer_count
    solved[layer_count - 1] = forward_list[layer_count - 1]
    for layer_idx in range(layer_count - 2, -1, -1):
        solved[layer_idx] = forward_list[layer_idx] - ratios[:, layer_idx] * solved[layer_idx + 1]
    line_value = jnp.stack(solved, 1)
    centre = vel_pad[:, :, 1:-1, 1:-1]
    return ice_cover * ((1.0 - OMEGA) * centre + OMEGA * line_value)


def lane_weights(comps, width):
    along_x = jnp.concatenate(
        [jnp.full((width,), (4.0, 1.0)[c], jnp.float32) for c in range(comps)]
    )
    along_y = jnp.concatenate(
        [jnp.full((width,), (1.0, 4.0)[c], jnp.float32) for c in range(comps)]
    )
    return (along_x, along_y)


def prepare_lanes(visc_pad, beta_col, ice_cover, weights):
    faces = lateral_terms(visc_pad)
    west_face, east_face, south_face, north_face = faces
    along_x, along_y = weights
    centre_visc = visc_pad[:, 1:-1, 1:-1]
    vertical = VERTICAL * 0.5 * (centre_visc[:-1] + centre_visc[1:])
    zero_row = jnp.zeros_like(centre_visc[:1])
    upper_link = jnp.concatenate([vertical, zero_row], 0)
    lower_link = jnp.concatenate([zero_row, vertical], 0)
    basal = jnp.concatenate([jnp.zeros_like(centre_visc[:-1]), beta_col[None]], 0)
    diagonal = along_x * (west_face + east_face) + along_y * (south_face + north_face)
    diagonal = diagonal + upper_link + lower_link + basal + (1.0 - ice_cover)
    layer_count = visc_pad.shape[0]
    ratio_list = []
    inverse_list = []
    for layer_idx in range(layer_count):
        pivot = diagonal[layer_idx]
        if layer_idx > 0:
            pivot = pivot + lower_link[layer_idx] * ratio_list[-1]
        inverse = 1.0 / pivot
        inverse_list.append(inverse)
        ratio_list.append(-upper_link[layer_idx] * inverse)
    return (faces, lower_link, ratio_list, inverse_list)


def relax_lanes(vel_pad, rhs_field, faces, lower_link, ratios, inverses, ice_cover, weights):
    west_face, east_face, south_face, north_face = faces
    along_x, along_y = weights
    lateral = along_x * (west_face * vel_pad[:, :-2, 1:-1] + east_face * vel_pad[:, 2:, 1:-1])
    lateral = lateral + along_y * (
        south_face * vel_pad[:, 1:-1, :-2] + north_face * vel_pad[:, 1:-1, 2:]
    )
    right_side = rhs_field + lateral
    layer_count = right_side.shape[0]
    forward_list = []
    for layer_idx in range(layer_count):
        value = right_side[layer_idx]
        if layer_idx > 0:
            value = value + lower_link[layer_idx] * forward_list[-1]
        forward_list.append(value * inverses[layer_idx])
    solved = [None] * layer_count
    solved[layer_count - 1] = forward_list[layer_count - 1]
    for layer_idx in range(layer_count - 2, -1, -1):
        solved[layer_idx] = forward_list[layer_idx] - ratios[layer_idx] * solved[layer_idx + 1]
    line_value = jnp.stack(solved, 0)
    centre = vel_pad[:, 1:-1, 1:-1]
    return ice_cover * ((1.0 - OMEGA) * centre + OMEGA * line_value)


def pad_cells(field):
    return jnp.pad(field, [(0, 0)] * (field.ndim - 2) + [(1, 1), (1, 1)])


def shifted(piece, axis, down):
    count = lax.axis_size(axis)
    if down:
        pairs = [(i, i + 1) for i in range(count - 1)]
    else:
        pairs = [(i + 1, i) for i in range(count - 1)]
    return lax.ppermute(piece, axis, pairs)


def local(forcing, viscosity, observed, beta_tiles, ice_mask, tile_owner):
    comps, layers, rows, cols = forcing.shape
    tiles_here = beta_tiles.shape[1]
    float_planes = [forcing.reshape(comps * layers, rows, cols), viscosity, observed]
    int_planes = [ice_mask[None], tile_owner[None]]

    def pieces(rows_at, cols_at):
        return [p[:, rows_at, cols_at] for p in float_planes] + [
            p[:, rows_at, cols_at].astype(jnp.float32) for p in int_planes
        ]

    plane_count = sum((p.shape[0] for p in float_planes + int_planes))
    every = slice(None)
    beta_plane = jnp.pad(beta_tiles, ((0, HALO - 1), (0, cols - tiles_here)))[None]
    head = jnp.concatenate(pieces(slice(0, HALO), every) + [beta_plane], axis=0)
    tail = jnp.concatenate(pieces(slice(rows - HALO, rows), every) + [beta_plane], axis=0)
    from_above = shifted(tail, "gx", True)
    from_below = shifted(head, "gx", False)

    def stack_rows(lo, hi):
        return jnp.concatenate(
            [from_above[:plane_count, :, lo:hi]]
            + [jnp.concatenate(pieces(every, slice(lo, hi)), axis=0)]
            + [from_below[:plane_count, :, lo:hi]],
            axis=1,
        )

    from_left = shifted(stack_rows(cols - HALO, cols), "gy", True)
    from_right = shifted(stack_rows(0, HALO), "gy", False)
    strips_near = jnp.stack(
        [
            from_above[plane_count, 0, :tiles_here],
            beta_tiles[0],
            from_below[plane_count, 0, :tiles_here],
        ]
    )
    friction_rows = lax.all_gather(strips_near, "gy", axis=1, tiled=True)
    tile_count = friction_rows.shape[1]
    packed = jnp.concatenate([from_left, stack_rows(0, cols), from_right], axis=2)
    ext_rows, ext_cols = (packed.shape[1], packed.shape[2])
    at = 0
    forcing_ext = packed[at : at + comps * layers].reshape(comps, layers, ext_rows, ext_cols)
    at += comps * layers
    visc_ext = packed[at : at + layers]
    at += layers
    observed_ext = packed[at : at + comps]
    at += comps
    ice_cover = packed[at]
    owner_ext = packed[at + 1].astype(jnp.int32)
    tiles = lax.broadcasted_iota(jnp.int32, (tile_count, 1, 1), 0)
    owner_match = owner_ext[None] == tiles
    row_strip = jnp.concatenate(
        [
            jnp.broadcast_to(friction_rows[0][:, None], (tile_count, HALO)),
            jnp.broadcast_to(friction_rows[1][:, None], (tile_count, rows)),
            jnp.broadcast_to(friction_rows[2][:, None], (tile_count, HALO)),
        ],
        axis=1,
    )
    beta_col = jnp.sum(jnp.where(owner_match, row_strip[:, :, None], 0.0), axis=0)

    def side_by_side(per_comp):
        return jnp.concatenate([per_comp[c] for c in range(comps)], axis=-1)

    weights = lane_weights(comps, ext_cols)
    visc_lanes = side_by_side([visc_ext] * comps)
    ice_lanes = side_by_side([ice_cover] * comps)
    beta_lanes = side_by_side([beta_col] * comps)
    forcing_lanes = side_by_side([forcing_ext[c] for c in range(comps)])
    observed_lanes = side_by_side([observed_ext[c] for c in range(comps)])
    faces, lower_link, ratios, inverses = prepare_lanes(
        pad_cells(visc_lanes), beta_lanes, ice_lanes, weights
    )

    def advance(field, rhs_field):
        return relax_lanes(
            pad_cells(field), rhs_field, faces, lower_link, ratios, inverses, ice_lanes, weights
        )

    velocity = jnp.zeros_like(forcing_lanes)
    for sweep_idx in range(PASSES):
        velocity = advance(velocity, forcing_lanes)
    misfit = velocity[0] - observed_lanes
    adjoint_rhs = jnp.zeros_like(forcing_lanes).at[0].set(misfit)
    adjoint = jnp.zeros_like(forcing_lanes)
    for sweep_idx in range(PASSES):
        adjoint = advance(adjoint, adjoint_rhs)
    inner = (slice(HALO, HALO + rows), slice(HALO, HALO + cols))

    def split(field):
        return jnp.stack(
            [
                field[:, inner[0], c * ext_cols + HALO : c * ext_cols + HALO + cols]
                for c in range(comps)
            ]
        )

    velocity = split(velocity)
    adjoint = split(adjoint)
    grad_col = (
        -ice_cover[inner] * beta_col[inner] * jnp.sum(adjoint[:, -1] * velocity[:, -1], axis=0)
    )
    high = lax.reduce_precision(grad_col, exponent_bits=8, mantissa_bits=7)
    rest = grad_col - high
    middle = lax.reduce_precision(rest, exponent_bits=8, mantissa_bits=7)
    low = rest - middle
    parts = jnp.stack([high, middle, low], axis=-1).reshape(rows * cols, 3).astype(jnp.bfloat16)
    block_match = tile_owner.reshape(rows * cols, 1) == lax.broadcasted_iota(
        jnp.int32, (1, tile_count), 1
    )
    per_part = lax.dot_general(
        block_match.astype(jnp.bfloat16),
        parts,
        (((0,), (0,)), ((), ())),
        preferred_element_type=jnp.float32,
    )
    partial_sum = per_part[:, 0] + per_part[:, 1] + per_part[:, 2]
    owners = lax.axis_size("gy")
    chunk = tile_count // owners
    gathered = lax.all_gather(partial_sum.reshape(owners, chunk), "gy")
    mine = lax.dynamic_index_in_dim(gathered, lax.axis_index("gy"), axis=1, keepdims=False)
    grad_tiles = jnp.sum(mine, axis=0)[None]
    return (velocity, adjoint, grad_tiles)


def solution(mesh):
    in_specs = (
        P(None, None, "gx", "gy"),
        P(None, "gx", "gy"),
        P(None, "gx", "gy"),
        P("gx", "gy"),
        P("gx", "gy"),
        P("gx", "gy"),
    )
    out_specs = (P(None, None, "gx", "gy"), P(None, None, "gx", "gy"), P("gx", "gy"))
    return jax.shard_map(local, mesh=mesh, in_specs=in_specs, out_specs=out_specs, check_vma=False)
```

profile of v0, /device:TPU:0, one launch (start us, length us, event | category | flops | bytes accessed | tf_op | source)
XLA Modules:
  0.0 61.5 jit_solution(2362320991496488223)
XLA Ops:
  0.7 1.0 %constant_dynamic-update-slice_fusion.5 = (f32[53,7,128]{2,1,0:T(8,128)S(1)}, f32[53,7,128]{2,1,0:T(8,128)S(1)}) fusion(f32[32,16,128]{2,1,0:T(8,128)} %bitcast.64), kind=kLoop, calls=%fused_computation.47 | loop fusion | bytes 491520
  1.7 0.9 %constant_dynamic-update-slice_fusion.4 = (f32[53,7,128]{2,1,0:T(8,128)S(1)}, f32[53,7,128]{2,1,0:T(8,128)S(1)}) fusion(f32[53,7,128]{2,1,0:T(8,128)S(1)} %get-tuple-element.252, f32[16,16,128]{2,1,0:T(8,128)} %param.9, f32[53,7,128]{2,1,0:T(8,128)S(1)} %get-tuple-element.253), kind=kLoop, calls=%fused_computation.46 | loop fusion | bytes 245760
  2.6 0.7 %constant_dynamic-update-slice_fusion.3 = (f32[53,7,128]{2,1,0:T(8,128)S(1)}, f32[53,7,128]{2,1,0:T(8,128)S(1)}) fusion(f32[53,7,128]{2,1,0:T(8,128)S(1)} %get-tuple-element.260, f32[2,16,128]{2,1,0:T(8,128)} %param.10, f32[53,7,128]{2,1,0:T(8,128)S(1)} %get-tuple-element.261), kind=kLoop, calls=%fused_computation.45 | loop fusion | bytes 30720
  3.3 0.7 %constant_dynamic-update-slice_fusion.2 = (f32[53,7,128]{2,1,0:T(8,128)S(1)}, f32[53,7,128]{2,1,0:T(8,128)S(1)}) fusion(f32[53,7,128]{2,1,0:T(8,128)S(1)} %get-tuple-element.271, s32[1,16,128]{2,1,0:T(8,128)} %bitcast.67, f32[53,7,128]{2,1,0:T(8,128)S(1)} %get-tuple-element.272), kind=kLoop, calls=%fused_computation.44 | loop fusion | flops 1792 | bytes 15360
  5.4 1.3 %collective-permute-start.1 = (f32[53,7,128]{2,1,0:T(8,128)S(1)}, f32[53,7,128]{2,1,0:T(8,128)S(1)}, u32[]{:S(2)}, u32[]{:S(2)}) collective-permute-start(f32[53,7,128]{2,1,0:T(8,128)S(1)} %get-tuple-element.287), channel_id=1, source_target_pairs={{8,0},{16,8},{24,16},{9,1},{17,9},{25,17},{10,2},{18,10},{26,18},{... | collective-permute-start | bytes 569864 | tf_op jit(solution)/shard_map/ppermute | solution.py:162
  6.7 5.6 %collective-permute-start = (f32[53,7,128]{2,1,0:T(8,128)S(1)}, f32[53,7,128]{2,1,0:T(8,128)S(1)}, u32[]{:S(2)}, u32[]{:S(2)}) collective-permute-start(f32[53,7,128]{2,1,0:T(8,128)S(1)} %get-tuple-element.286), channel_id=1, source_target_pairs={{0,8},{8,16},{16,24},{1,9},{9,17},{17,25},{2,10},{10,18},{18,26},{... | collective-permute-start | bytes 569864 | tf_op jit(solution)/shard_map/ppermute | solution.py:162
  12.3 1.2 %fusion.298 = (f32[32,16,7]{2,1,0:T(8,128)S(1)}, f32[32,16,7]{2,1,0:T(8,128)S(1)}) fusion(f32[32,16,128]{2,1,0:T(8,128)} %bitcast.65), kind=kLoop, calls=%fused_computation.671 | loop fusion | bytes 57344 | tf_op jit(solution)/shard_map/slice | solution.py:172
  17.2 1.3 %collective-permute-start.3 = (f32[52,30,7]{0,1,2:T(8,128)S(1)}, f32[52,30,7]{0,1,2:T(8,128)S(1)}, u32[]{:S(2)}, u32[]{:S(2)}) collective-permute-start(f32[52,30,7]{0,1,2:T(8,128)S(1)} %pad_maximum_fusion.6), channel_id=1, source_target_pairs={{1,0},{2,1},{3,2},{4,3},{5,4},{6,5},{7,6},{9,8},{10,9},{11,10},{12... | collective-permute-start | bytes 131048 | tf_op jit(solution)/shard_map/ppermute | solution.py:162
  18.8 3.0 %collective-permute-start.2 = (f32[52,30,7]{0,1,2:T(8,128)S(1)}, f32[52,30,7]{0,1,2:T(8,128)S(1)}, u32[]{:S(2)}, u32[]{:S(2)}) collective-permute-start(f32[52,30,7]{0,1,2:T(8,128)S(1)} %pad_maximum_fusion.5), channel_id=1, source_target_pairs={{0,1},{1,2},{2,3},{3,4},{4,5},{5,6},{6,7},{8,9},{9,10},{10,11},{11... | collective-permute-start | bytes 131048 | tf_op jit(solution)/shard_map/ppermute | solution.py:162
  21.9 9.2 %all-gather = f32[8,16,3]{1,2,0:T(4,128)S(1)} all-gather(f32[1,16,3]{1,2,0:T(4,128)S(1)} %maximum_bitcast_fusion.2), channel_id=1, replica_groups=mesh['gx'=4,'gy'=8] {'gy'}, dimensions={0}, use_global_device_ids=true | all-gather | bytes 1728 | tf_op jit(solution)/shard_map/all_gather | solution.py:201
  31.3 0.8 %copy.65 = f32[52,30,7]{2,1,0:T(8,128)S(1)} copy(f32[52,30,7]{0,1,2:T(8,128)S(1)} %collective-permute-done.3) | data formatting | bytes 87360 | tf_op jit(solution)/shard_map/ppermute | solution.py:162
  32.2 0.9 %copy.64 = f32[52,30,7]{2,1,0:T(8,128)S(1)} copy(f32[52,30,7]{0,1,2:T(8,128)S(1)} %collective-permute-done.2) | data formatting | bytes 87360 | tf_op jit(solution)/shard_map/ppermute | solution.py:162
  33.0 1.0 %pad_maximum_fusion = f32[52,30,142]{2,1,0:T(8,128)S(1)} fusion(f32[52,30,7]{2,1,0:T(8,128)S(1)} %copy.65, f32[52,7,128]{2,1,0:T(8,128)S(1)} %slice.1159, f32[52,16,128]{2,1,0:T(8,128)S(1)} %constant_dynamic-update-slice_fusion.12, f32[52,7,128]{2,1,0:T(8,128)S(1)} %slice.1158, f32[52,30,7]{2,1,0:T(8,128)S(1)} %copy.64), kind=kLoop, calls=%fused_computation.2 | loop fusion | flops 886080 | bytes 1772160 | tf_op jit(solution)/shard_map/concatenate | solution.py:203
  34.8 2.2 %select_reduce_fusion = f32[30,142]{1,0:T(8,128)S(1)} fusion(f32[128,30]{0,1:T(8,128)S(1)} %pad_maximum_fusion.16, s32[30,142]{1,0:T(8,128)S(1)} %get-tuple-element.242), kind=kLoop, calls=%fused_computation | loop fusion | flops 1631580 | bytes 49440 | tf_op jit(solution)/shard_map/reduce_sum | solution.py:224
  37.2 0.8 %fusion.167 = (f32[16,30,284]{2,1,0:T(8,128)S(1)}, f32[16,30,284]{2,1,0:T(8,128)S(1)}, f32[16,30,284]{2,1,0:T(8,128)S(1)}, f32[16,30,284]{2,1,0:T(8,128)S(1)}, f...) fusion(f32[16,30,142]{2,1,0:T(8,128)S(1)} %get-tuple-element.244, f32[16,30,142]{2,1,0:T(8,128)S(1)} %get-tuple-element.245, ...), kind=kLoop, calls=%fused_computation.669 | loop fusion | flops 2044800 | bytes 4500832 | tf_op jit(solution)/shard_map/add | solution.py:135
  39.3 0.9 %add_add_fusion.2 = f32[16,30,284]{2,1,0:T(8,128)S(1)} fusion(f32[16,30,284]{2,1,0:T(8,128)S(1)} %broadcast_multiply_fusion.1, f32[16,30,284]{2,1,0:T(8,128)S(1)} %get-tuple-element.240, f32[16,30,284]{2,1,0:T(8,128)S(1)} %get-tuple-element.239, f32[16,30,284]{2,1,0:T(8,128)S(1)} %get-tuple-element.238, f32[16,30,284]{2,1,0:T(8,128)S(1)} %get-tuple-element.237, ...), kind=kLoop, calls=%fused_computation.22 | loop fusion | flops 2044800 | bytes 3819232 | tf_op jit(solution)/shard_map/add | solution.py:135
  40.9 0.9 %add_add_fusion.1 = f32[16,30,284]{2,1,0:T(8,128)S(1)} fusion(f32[16,30,284]{2,1,0:T(8,128)S(1)} %add_multiply_fusion.5, f32[16,30,284]{2,1,0:T(8,128)S(1)} %get-tuple-element.240, f32[16,30,284]{2,1,0:T(8,128)S(1)} %get-tuple-element.239, f32[16,30,284]{2,1,0:T(8,128)S(1)} %get-tuple-element.238, f32[16,30,284]{2,1,0:T(8,128)S(1)} %get-tuple-element.237, ...), kind=kLoop, calls=%fused_computation.20 | loop fusion | flops 2044800 | bytes 3819232 | tf_op jit(solution)/shard_map/add | solution.py:135
  42.6 0.9 %add_add_fusion = f32[16,30,284]{2,1,0:T(8,128)S(1)} fusion(f32[16,30,284]{2,1,0:T(8,128)S(1)} %add_multiply_fusion.4, f32[16,30,284]{2,1,0:T(8,128)S(1)} %get-tuple-element.240, f32[16,30,284]{2,1,0:T(8,128)S(1)} %get-tuple-element.239, f32[16,30,284]{2,1,0:T(8,128)S(1)} %get-tuple-element.238, f32[16,30,284]{2,1,0:T(8,128)S(1)} %get-tuple-element.237, ...), kind=kLoop, calls=%fused_computation.18 | loop fusion | flops 2044800 | bytes 3819232 | tf_op jit(solution)/shard_map/add | solution.py:135
  44.9 0.8 %multiply_add_fusion.2 = f32[16,30,284]{2,1,0:T(8,128)S(1)} fusion(f32[16,30,284]{2,1,0:T(8,128)S(1)} %broadcast_multiply_fusion, f32[16,30,284]{2,1,0:T(8,128)S(1)} %get-tuple-element.240, f32[16,30,284]{2,1,0:T(8,128)S(1)} %get-tuple-element.239, f32[16,30,284]{2,1,0:T(8,128)S(1)} %get-tuple-element.238, f32[16,30,284]{2,1,0:T(8,128)S(1)} %get-tuple-element.237, ...), kind=kLoop, calls=%fused_computation.16 | loop fusion | flops 1772160 | bytes 3273952 | tf_op jit(solution)/shard_map/add | solution.py:132
  46.5 0.8 %multiply_add_fusion.1 = f32[16,30,284]{2,1,0:T(8,128)S(1)} fusion(f32[16,30,284]{2,1,0:T(8,128)S(1)} %add_multiply_fusion.2, f32[16,30,284]{2,1,0:T(8,128)S(1)} %get-tuple-element.240, f32[16,30,284]{2,1,0:T(8,128)S(1)} %get-tuple-element.239, f32[16,30,284]{2,1,0:T(8,128)S(1)} %get-tuple-element.238, f32[16,30,284]{2,1,0:T(8,128)S(1)} %get-tuple-element.237, ...), kind=kLoop, calls=%fused_computation.14 | loop fusion | flops 1772160 | bytes 3273952 | tf_op jit(solution)/shard_map/add | solution.py:132
  48.0 0.8 %multiply_add_fusion = f32[16,30,284]{2,1,0:T(8,128)S(1)} fusion(f32[16,30,284]{2,1,0:T(8,128)S(1)} %add_multiply_fusion.1, f32[16,30,284]{2,1,0:T(8,128)S(1)} %get-tuple-element.240, f32[16,30,284]{2,1,0:T(8,128)S(1)} %get-tuple-element.239, f32[16,30,284]{2,1,0:T(8,128)S(1)} %get-tuple-element.238, f32[16,30,284]{2,1,0:T(8,128)S(1)} %get-tuple-element.237, ...), kind=kLoop, calls=%fused_computation.12 | loop fusion | flops 1772160 | bytes 3273952 | tf_op jit(solution)/shard_map/add | solution.py:132
  49.8 0.7 %pad_maximum_fusion.3 = f32[2,16,16,128]{3,2,1,0:T(8,128)} fusion(f32[1,16,16,128]{3,2,1,0:T(8,128)S(1)} %get-tuple-element.288, f32[1,16,16,128]{3,2,1,0:T(8,128)S(1)} %get-tuple-element.289), kind=kLoop, calls=%fused_computation.37 | loop fusion | flops 65536 | bytes 524288 | tf_op jit(solution)/shard_map/stack | solution.py:255
  50.5 0.7 %pad_maximum_fusion.4 = f32[2,16,16,128]{3,2,1,0:T(8,128)} fusion(f32[1,16,16,128]{3,2,1,0:T(8,128)S(1)} %get-tuple-element.247, f32[1,16,16,128]{3,2,1,0:T(8,128)S(1)} %get-tuple-element.246), kind=kLoop, calls=%fused_computation.40 | loop fusion | flops 65536 | bytes 524288 | tf_op jit(solution)/shard_map/stack | solution.py:255
  51.9 9.1 %all_gather.7 = f32[8,8,16]{2,1,0:T(8,128)S(1)} all-gather(f32[1,8,16]{2,1,0:T(8,128)S(1)} %add.4639), channel_id=1, replica_groups=mesh['gx'=4,'gy'=8] {'gy'}, dimensions={0}, use_global_device_ids=true | all-gather | bytes 4608 | tf_op jit(solution)/shard_map/all_gather | solution.py:284
  (227 shorter events, 13.3 us)
Async XLA Ops:
  0.6 13.2 %copy-start = (f32[2,16,16,128]{3,2,1,0:T(8,128)S(1)}, f32[2,16,16,128]{3,2,1,0:T(8,128)}, u32[]{:S(2)}) copy-start(f32[2,16,16,128]{3,2,1,0:T(8,128)} %param.8) | copy-start | bytes 786436
  0.6 12.8 %copy-start.1 = (f32[16,16,128]{2,1,0:T(8,128)S(1)}, f32[16,16,128]{2,1,0:T(8,128)}, u32[]{:S(2)}) copy-start(f32[16,16,128]{2,1,0:T(8,128)} %param.9) | copy-start | bytes 393220
  0.7 12.9 %copy-start.2 = (f32[2,16,128]{2,1,0:T(8,128)S(1)}, f32[2,16,128]{2,1,0:T(8,128)}, u32[]{:S(2)}) copy-start(f32[2,16,128]{2,1,0:T(8,128)} %param.10) | copy-start | bytes 49156
  0.7 13.0 %copy-start.5 = (s32[16,128]{1,0:T(8,128)S(1)}, s32[16,128]{1,0:T(8,128)}, u32[]{:S(2)}) copy-start(s32[16,128]{1,0:T(8,128)} %param.12) | copy-start | bytes 24580
  0.7 13.0 %copy-start.6 = (s32[16,128]{1,0:T(8,128)S(1)}, s32[16,128]{1,0:T(8,128)}, u32[]{:S(2)}) copy-start(s32[16,128]{1,0:T(8,128)} %param.13) | copy-start | bytes 24580
  5.4 11.0 %collective-permute-start.1 = (f32[53,7,128]{2,1,0:T(8,128)S(1)}, f32[53,7,128]{2,1,0:T(8,128)S(1)}, u32[]{:S(2)}, u32[]{:S(2)}) collective-permute-start(f32[53,7,128]{2,1,0:T(8,128)S(1)} %get-tuple-element.287), channel_id=1, source_target_pairs={{8,0},{16,8},{24,16},{9,1},{17,9},{25,17},{10,2},{18,10},{26,18},{... | collective-permute-start | bytes 569864 | tf_op jit(solution)/shard_map/ppermute | solution.py:162
  6.7 10.1 %collective-permute-start = (f32[53,7,128]{2,1,0:T(8,128)S(1)}, f32[53,7,128]{2,1,0:T(8,128)S(1)}, u32[]{:S(2)}, u32[]{:S(2)}) collective-permute-start(f32[53,7,128]{2,1,0:T(8,128)S(1)} %get-tuple-element.286), channel_id=1, source_target_pairs={{0,8},{8,16},{16,24},{1,9},{9,17},{17,25},{2,10},{10,18},{18,26},{... | collective-permute-start | bytes 569864 | tf_op jit(solution)/shard_map/ppermute | solution.py:162
  16.2 5.7 %copy-start.7 = (f32[1,16]{1,0:T(1,128)S(1)}, f32[1,16]{1,0:T(1,128)}, u32[]{:S(2)}) copy-start(f32[1,16]{1,0:T(1,128)} %param.11) | copy-start | bytes 196
  17.2 14.1 %collective-permute-start.3 = (f32[52,30,7]{0,1,2:T(8,128)S(1)}, f32[52,30,7]{0,1,2:T(8,128)S(1)}, u32[]{:S(2)}, u32[]{:S(2)}) collective-permute-start(f32[52,30,7]{0,1,2:T(8,128)S(1)} %pad_maximum_fusion.6), channel_id=1, source_target_pairs={{1,0},{2,1},{3,2},{4,3},{5,4},{6,5},{7,6},{9,8},{10,9},{11,10},{12... | collective-permute-start | bytes 131048 | tf_op jit(solution)/shard_map/ppermute | solution.py:162
  18.8 13.3 %collective-permute-start.2 = (f32[52,30,7]{0,1,2:T(8,128)S(1)}, f32[52,30,7]{0,1,2:T(8,128)S(1)}, u32[]{:S(2)}, u32[]{:S(2)}) collective-permute-start(f32[52,30,7]{0,1,2:T(8,128)S(1)} %pad_maximum_fusion.5), channel_id=1, source_target_pairs={{0,1},{1,2},{2,3},{3,4},{4,5},{5,6},{6,7},{8,9},{9,10},{10,11},{11... | collective-permute-start | bytes 131048 | tf_op jit(solution)/shard_map/ppermute | solution.py:162
  34.7 2.5 %copy-start.3 = (f32[284]{0:T(512)S(1)}, f32[284]{0:T(512)}, u32[]{:S(2)}) copy-start(f32[284]{0:T(512)} %constant.51.clone.1) | copy-start | bytes 3412
  34.7 2.5 %copy-start.4 = (f32[284]{0:T(512)S(1)}, f32[284]{0:T(512)}, u32[]{:S(2)}) copy-start(f32[284]{0:T(512)} %constant.49.clone.1) | copy-start | bytes 3412
where the time goes:
time: 62 us; the launch traced here: 61.5 us
  other arithmetic  18.8 us (30%)
  blocking collectives  18.3 us (30%)
  starting transfers between devices  11.2 us (18%)
  local copies, waits for them, and re-layouts  10.6 us (17%)
  between operations  2.09 us (3%)
    ppermute x4, starting transfers between devices, shifted(): return lax.ppermute(piece, axis, pairs)  11.2 us
    all_gather x1, blocking collectives, local(): friction_rows = lax.all_gather(strips_near, 'gy', axis=1, tiled=True)  9.2 us
    all_gather x1, blocking collectives, local(): gathered = lax.all_gather(partial_sum.reshape(owners, chunk), 'gy')  9.05 us
    unnamed x86, local copies, waits for them, and re-layouts  4.03 us
    add x4, other arithmetic, relax_lanes(): right_side = rhs_field + lateral  3.52 us
    unnamed x70, other arithmetic  3.46 us
    add x3, other arithmetic, relax_lanes(): lateral + along_y * (south_face * vel_pad[:, 1:-1, :-2] + north_face * ve...  2.35 us
    reduce_sum x1, other arithmetic, local(): jnp.sum(jnp.where(owner_match, row_strip[:, :, None], 0.0), axis=0)  2.23 us
  transfers between devices with their start and end apart: 4, of which 1 were waited for; matrix products, arithmetic and copies ran while one was open for 9% of the time, Pallas kernels for 0%

commit v1 on v0

--- a/solution.py
+++ b/solution.py
@@ -198,7 +198,26 @@
             from_below[plane_count, 0, :tiles_here],
         ]
     )
-    friction_rows = lax.all_gather(strips_near, "gy", axis=1, tiled=True)
+    res = lax.axis_size("gy")
+    front = lax.axis_index("gy")
+    prior, t1, val = (res, front, strips_near.shape[1])
+    all_blocks = [dd * prior if q == 1 else dd for q, dd in enumerate(strips_near.shape)]
+    friction_rows = lax.dynamic_update_slice_in_dim(
+        jnp.zeros(all_blocks, strips_near.dtype), strips_near, t1 * val, axis=1
+    )
+    x_now = block_next = strips_near
+    for idx in range(1, prior // 2 + 1):
+        x_now = lax.ppermute(x_now, "gy", [(q, (q + 1) % prior) for q in range(prior)])
+        friction_rows = lax.dynamic_update_slice_in_dim(
+            friction_rows, x_now, (t1 - idx) % prior * val, axis=1
+        )
+        if 2 * idx < prior:
+            block_next = lax.ppermute(
+                block_next, "gy", [(q, (q - 1) % prior) for q in range(prior)]
+            )
+            friction_rows = lax.dynamic_update_slice_in_dim(
+                friction_rows, block_next, (t1 + idx) % prior * val, axis=1
+            )
     tile_count = friction_rows.shape[1]
     packed = jnp.concatenate([from_left, stack_rows(0, cols), from_right], axis=2)
     ext_rows, ext_cols = (packed.shape[1], packed.shape[2])

time: 62 us -> 70.6 us (1.14)
  blocking collectives: 18.3 us -> 11 us
  starting transfers between devices: 11.2 us -> 17.1 us
  waiting for transfers between devices: 0.18 us -> 5.98 us
  local copies, waits for them, and re-layouts: 10.6 us -> 12.9 us
  other arithmetic: 18.8 us -> 20.3 us
    all_gather x1 -> x0, blocking collectives: 9.2 us -> none  [local(): friction_rows = lax.all_gather(strips_near, 'gy', axis=1, tiled=True)]
    ppermute x0 -> x7, starting transfers between devices: none -> 6.24 us  [the longest x3 4.35 us: local(): lax.ppermute(block_next, 'gy', [(q, (q - 1) % prior) for q in range(prior)])]
    ppermute x0 -> x7, waiting for transfers between devices: none -> 5.22 us  [the longest x4 5.17 us: local(): lax.ppermute(x_now, 'gy', [(q, (q + 1) % prior) for q in range(prior)])]
    all_gather x1, blocking collectives: 9.05 us -> 11 us  [local(): gathered = lax.all_gather(partial_sum.reshape(owners, chunk), 'gy')]
    dynamic_update_slice x0 -> x8, local copies, waits for them, and re-layouts: none -> 1.59 us  [the longest x4 0.75 us: local(): lax.dynamic_update_slice_in_dim(friction_rows, x_now, (t1 - idx) % prior...]
    convert_element_type x2, other arithmetic: 0.15 us -> 1.69 us  [pieces(): p[:, rows_at, cols_at].astype(jnp.float32)]
    slice x5, local copies, waits for them, and re-layouts: 1.71 us -> 2.47 us  [pieces(): p[:, rows_at, cols_at]]
    unnamed x86 -> x85, local copies, waits for them, and re-layouts: 4.03 us -> 3.93 us
  transfers between devices with their start and end apart: 4 -> 11, of which waited for: 1 -> 4; matrix products, arithmetic and copies ran while one was open for 9% -> 14% of each run, Pallas kernels for 0% -> 0%
where the time goes in v1:
time: 70.6 us; the launch traced here: 69.9 us
  other arithmetic  20.3 us (29%)
  starting transfers between devices  17.1 us (24%)
  local copies, waits for them, and re-layouts  12.9 us (18%)
  blocking collectives  11 us (16%)
  waiting for transfers between devices  5.98 us (8%)
  between operations  2.27 us (3%)
    all_gather x1, blocking collectives, local(): gathered = lax.all_gather(partial_sum.reshape(owners, chunk), 'gy')  11 us
    ppermute x4, starting transfers between devices, shifted(): return lax.ppermute(piece, axis, pairs)  10.8 us
    ppermute x4, waiting for transfers between devices, local(): lax.ppermute(x_now, 'gy', [(q, (q + 1) % prior) for q in range(prior)])  5.17 us
    ppermute x3, starting transfers between devices, local(): lax.ppermute(block_next, 'gy', [(q, (q - 1) % prior) for q in range(prior)])  4.35 us
    unnamed x85, local copies, waits for them, and re-layouts  3.93 us
    add x4, other arithmetic, relax_lanes(): right_side = rhs_field + lateral  3.52 us
    unnamed x69, other arithmetic  3.45 us
    slice x5, local copies, waits for them, and re-layouts, pieces(): p[:, rows_at, cols_at]  2.47 us
  transfers between devices with their start and end apart: 11, of which 4 were waited for; matrix products, arithmetic and copies ran while one was open for 14% of the time, Pallas kernels for 0%

profile of v1, /device:TPU:0, one launch (start us, length us, event | category | flops | bytes accessed | tf_op | source)
XLA Modules:
  0.0 69.9 jit_solution(16987477889107131573)
XLA Ops:
  0.6 1.0 %constant_dynamic-update-slice_fusion.5 = (f32[53,7,128]{2,1,0:T(8,128)S(1)}, f32[53,7,128]{2,1,0:T(8,128)S(1)}) fusion(f32[32,16,128]{2,1,0:T(8,128)} %bitcast.57), kind=kLoop, calls=%fused_computation.47 | loop fusion | bytes 491520
  1.7 0.9 %constant_dynamic-update-slice_fusion.4 = (f32[53,7,128]{2,1,0:T(8,128)S(1)}, f32[53,7,128]{2,1,0:T(8,128)S(1)}) fusion(f32[53,7,128]{2,1,0:T(8,128)S(1)} %get-tuple-element.252, f32[16,16,128]{2,1,0:T(8,128)} %param.9, f32[53,7,128]{2,1,0:T(8,128)S(1)} %get-tuple-element.253), kind=kLoop, calls=%fused_computation.46 | loop fusion | bytes 245760
  5.4 4.9 %collective-permute-start = (f32[53,7,128]{2,1,0:T(8,128)S(1)}, f32[53,7,128]{2,1,0:T(8,128)S(1)}, u32[]{:S(2)}, u32[]{:S(2)}) collective-permute-start(f32[53,7,128]{2,1,0:T(8,128)S(1)} %get-tuple-element.286), channel_id=1, source_target_pairs={{0,8},{8,16},{16,24},{1,9},{9,17},{17,25},{2,10},{10,18},{18,26},{... | collective-permute-start | bytes 569864 | tf_op jit(solution)/shard_map/ppermute | solution.py:162
  10.3 1.3 %collective-permute-start.1 = (f32[53,7,128]{2,1,0:T(8,128)S(1)}, f32[53,7,128]{2,1,0:T(8,128)S(1)}, u32[]{:S(2)}, u32[]{:S(2)}) collective-permute-start(f32[53,7,128]{2,1,0:T(8,128)S(1)} %get-tuple-element.287), channel_id=1, source_target_pairs={{8,0},{16,8},{24,16},{9,1},{17,9},{25,17},{10,2},{18,10},{26,18},{... | collective-permute-start | bytes 569864 | tf_op jit(solution)/shard_map/ppermute | solution.py:162
  11.7 0.8 %slice_convert_fusion.3 = (f32[1,16,7]{2,1,0:T(8,128)S(1)}, f32[1,16,7]{2,1,0:T(8,128)S(1)}) fusion(s32[1,16,128]{2,1,0:T(8,128)} %bitcast.61), kind=kLoop, calls=%fused_computation.652 | loop fusion | flops 224 | bytes 1792 | tf_op jit(solution)/shard_map/convert_element_type | solution.py:173
  12.6 0.8 %slice_convert_fusion.2 = (f32[1,16,7]{2,1,0:T(8,128)S(1)}, f32[1,16,7]{2,1,0:T(8,128)S(1)}) fusion(s32[1,16,128]{2,1,0:T(8,128)} %bitcast.63), kind=kLoop, calls=%fused_computation.651 | loop fusion | flops 224 | bytes 1792 | tf_op jit(solution)/shard_map/convert_element_type | solution.py:173
  13.4 0.9 %fusion.302 = (f32[2,16,7]{2,1,0:T(8,128)S(1)}, f32[2,16,7]{2,1,0:T(8,128)S(1)}) fusion(f32[2,16,128]{2,1,0:T(8,128)} %param.10), kind=kLoop, calls=%fused_computation.675 | loop fusion | bytes 3584 | tf_op jit(solution)/shard_map/slice | solution.py:172
  14.3 1.1 %fusion.301 = (f32[16,16,7]{2,1,0:T(8,128)S(1)}, f32[16,16,7]{2,1,0:T(8,128)S(1)}) fusion(f32[16,16,128]{2,1,0:T(8,128)} %param.9), kind=kLoop, calls=%fused_computation.674 | loop fusion | bytes 28672 | tf_op jit(solution)/shard_map/slice | solution.py:172
  19.0 0.9 %collective-permute-start.5 = (f32[3,16]{1,0:T(4,128)S(1)}, f32[3,16]{1,0:T(4,128)S(1)}, u32[]{:S(2)}, u32[]{:S(2)}) collective-permute-start(f32[3,16]{1,0:T(4,128)S(1)} %pad_maximum_fusion.17), channel_id=1, source_target_pairs={{0,7},{1,0},{2,1},{3,2},{4,3},{5,4},{6,5},{7,6},{8,15},{9,8},{10,9... | collective-permute-start | bytes 584 | tf_op jit(solution)/shard_map/ppermute | solution.py:215
  20.9 1.3 %collective-permute-start.3 = (f32[52,30,7]{0,1,2:T(8,128)S(1)}, f32[52,30,7]{0,1,2:T(8,128)S(1)}, u32[]{:S(2)}, u32[]{:S(2)}) collective-permute-start(f32[52,30,7]{0,1,2:T(8,128)S(1)} %pad_maximum_fusion.6), channel_id=1, source_target_pairs={{1,0},{2,1},{3,2},{4,3},{5,4},{6,5},{7,6},{9,8},{10,9},{11,10},{12... | collective-permute-start | bytes 131048 | tf_op jit(solution)/shard_map/ppermute | solution.py:162
  22.2 3.3 %collective-permute-start.2 = (f32[52,30,7]{0,1,2:T(8,128)S(1)}, f32[52,30,7]{0,1,2:T(8,128)S(1)}, u32[]{:S(2)}, u32[]{:S(2)}) collective-permute-start(f32[52,30,7]{0,1,2:T(8,128)S(1)} %pad_maximum_fusion.5), channel_id=1, source_target_pairs={{0,1},{1,2},{2,3},{3,4},{4,5},{5,6},{6,7},{8,9},{9,10},{10,11},{11... | collective-permute-start | bytes 131048 | tf_op jit(solution)/shard_map/ppermute | solution.py:162
  25.8 1.9 %collective-permute-start.6 = (f32[3,16]{1,0:T(4,128)S(1)}, f32[3,16]{1,0:T(4,128)S(1)}, u32[]{:S(2)}, u32[]{:S(2)}) collective-permute-start(f32[3,16]{1,0:T(4,128)S(1)} %collective-permute-done.4), channel_id=1, source_target_pairs={{0,1},{1,2},{2,3},{3,4},{4,5},{5,6},{6,7},{7,0},{8,9},{9,10},{10,1... | collective-permute-start | bytes 584 | tf_op jit(solution)/shard_map/ppermute | solution.py:210
  28.9 0.9 %collective-permute-done.6 = f32[3,16]{1,0:T(4,128)S(1)} collective-permute-done((f32[3,16]{1,0:T(4,128)S(1)}, f32[3,16]{1,0:T(4,128)S(1)}, u32[]{:S(2)}, u32[]{:S(2)}) %collective-permute-start.6) | collective-permute-done | bytes 224 | tf_op jit(solution)/shard_map/ppermute | solution.py:210
  29.8 2.6 %collective-permute-start.9 = (f32[3,16]{1,0:T(4,128)S(1)}, f32[3,16]{1,0:T(4,128)S(1)}, u32[]{:S(2)}, u32[]{:S(2)}) collective-permute-start(f32[3,16]{1,0:T(4,128)S(1)} %collective-permute-done.7), channel_id=1, source_target_pairs={{0,7},{1,0},{2,1},{3,2},{4,3},{5,4},{6,5},{7,6},{8,15},{9,8},{10,9... | collective-permute-start | bytes 584 | tf_op jit(solution)/shard_map/ppermute | solution.py:215
  32.8 0.9 %collective-permute-done.8 = f32[3,16]{1,0:T(4,128)S(1)} collective-permute-done((f32[3,16]{1,0:T(4,128)S(1)}, f32[3,16]{1,0:T(4,128)S(1)}, u32[]{:S(2)}, u32[]{:S(2)}) %collective-permute-start.8) | collective-permute-done | bytes 224 | tf_op jit(solution)/shard_map/ppermute | solution.py:210
  34.1 3.5 %collective-permute-done.10 = f32[3,16]{1,0:T(4,128)S(1)} collective-permute-done((f32[3,16]{1,0:T(4,128)S(1)}, f32[3,16]{1,0:T(4,128)S(1)}, u32[]{:S(2)}, u32[]{:S(2)}) %collective-permute-start.10) | collective-permute-done | bytes 224 | tf_op jit(solution)/shard_map/ppermute | solution.py:210
  37.8 0.8 %copy.61 = f32[52,30,7]{2,1,0:T(8,128)S(1)} copy(f32[52,30,7]{0,1,2:T(8,128)S(1)} %collective-permute-done.2) | data formatting | bytes 87360 | tf_op jit(solution)/shard_map/ppermute | solution.py:162
  38.7 0.9 %copy.62 = f32[52,30,7]{2,1,0:T(8,128)S(1)} copy(f32[52,30,7]{0,1,2:T(8,128)S(1)} %collective-permute-done.3) | data formatting | bytes 87360 | tf_op jit(solution)/shard_map/ppermute | solution.py:162
  39.6 1.0 %pad_maximum_fusion = f32[52,30,142]{2,1,0:T(8,128)S(1)} fusion(f32[52,30,7]{2,1,0:T(8,128)S(1)} %copy.62, f32[52,7,128]{2,1,0:T(8,128)S(1)} %slice.1159, f32[52,16,128]{2,1,0:T(8,128)S(1)} %constant_dynamic-update-slice_fusion.12, f32[52,7,128]{2,1,0:T(8,128)S(1)} %slice.1158, f32[52,30,7]{2,1,0:T(8,128)S(1)} %copy.61), kind=kLoop, calls=%fused_computation.2 | loop fusion | flops 886080 | bytes 1772160 | tf_op jit(solution)/shard_map/concatenate | solution.py:222
  41.3 2.2 %select_reduce_fusion = f32[30,142]{1,0:T(8,128)S(1)} fusion(f32[128,30]{0,1:T(8,128)S(1)} %pad_maximum_fusion.16, s32[30,142]{1,0:T(8,128)S(1)} %get-tuple-element.242), kind=kLoop, calls=%fused_computation | loop fusion | flops 1631580 | bytes 49440 | tf_op jit(solution)/shard_map/reduce_sum | solution.py:243
  45.7 0.9 %add_add_fusion.2 = f32[16,30,284]{2,1,0:T(8,128)S(1)} fusion(f32[16,30,284]{2,1,0:T(8,128)S(1)} %broadcast_multiply_fusion.1, f32[16,30,284]{2,1,0:T(8,128)S(1)} %get-tuple-element.240, f32[16,30,284]{2,1,0:T(8,128)S(1)} %get-tuple-element.239, f32[16,30,284]{2,1,0:T(8,128)S(1)} %get-tuple-element.238, f32[16,30,284]{2,1,0:T(8,128)S(1)} %get-tuple-element.237, ...), kind=kLoop, calls=%fused_computation.22 | loop fusion | flops 2044800 | bytes 3819232 | tf_op jit(solution)/shard_map/add | solution.py:135
  47.4 0.9 %add_add_fusion.1 = f32[16,30,284]{2,1,0:T(8,128)S(1)} fusion(f32[16,30,284]{2,1,0:T(8,128)S(1)} %add_multiply_fusion.5, f32[16,30,284]{2,1,0:T(8,128)S(1)} %get-tuple-element.240, f32[16,30,284]{2,1,0:T(8,128)S(1)} %get-tuple-element.239, f32[16,30,284]{2,1,0:T(8,128)S(1)} %get-tuple-element.238, f32[16,30,284]{2,1,0:T(8,128)S(1)} %get-tuple-element.237, ...), kind=kLoop, calls=%fused_computation.20 | loop fusion | flops 2044800 | bytes 3819232 | tf_op jit(solution)/shard_map/add | solution.py:135
  49.0 0.9 %add_add_fusion = f32[16,30,284]{2,1,0:T(8,128)S(1)} fusion(f32[16,30,284]{2,1,0:T(8,128)S(1)} %add_multiply_fusion.4, f32[16,30,284]{2,1,0:T(8,128)S(1)} %get-tuple-element.240, f32[16,30,284]{2,1,0:T(8,128)S(1)} %get-tuple-element.239, f32[16,30,284]{2,1,0:T(8,128)S(1)} %get-tuple-element.238, f32[16,30,284]{2,1,0:T(8,128)S(1)} %get-tuple-element.237, ...), kind=kLoop, calls=%fused_computation.18 | loop fusion | flops 2044800 | bytes 3819232 | tf_op jit(solution)/shard_map/add | solution.py:135
  58.4 11.0 %all_gather.3 = f32[8,8,16]{2,1,0:T(8,128)S(1)} all-gather(f32[1,8,16]{2,1,0:T(8,128)S(1)} %add.4716), channel_id=1, replica_groups=mesh['gx'=4,'gy'=8] {'gy'}, dimensions={0}, use_global_device_ids=true | all-gather | bytes 4608 | tf_op jit(solution)/shard_map/all_gather | solution.py:303
  (247 shorter events, 22.1 us)
Async XLA Ops:
  0.6 14.8 %copy-start = (f32[2,16,16,128]{3,2,1,0:T(8,128)S(1)}, f32[2,16,16,128]{3,2,1,0:T(8,128)}, u32[]{:S(2)}) copy-start(f32[2,16,16,128]{3,2,1,0:T(8,128)} %param.8) | copy-start | bytes 786436
  5.4 12.9 %collective-permute-start = (f32[53,7,128]{2,1,0:T(8,128)S(1)}, f32[53,7,128]{2,1,0:T(8,128)S(1)}, u32[]{:S(2)}, u32[]{:S(2)}) collective-permute-start(f32[53,7,128]{2,1,0:T(8,128)S(1)} %get-tuple-element.286), channel_id=1, source_target_pairs={{0,8},{8,16},{16,24},{1,9},{9,17},{17,25},{2,10},{10,18},{18,26},{... | collective-permute-start | bytes 569864 | tf_op jit(solution)/shard_map/ppermute | solution.py:162
  10.3 8.7 %collective-permute-start.1 = (f32[53,7,128]{2,1,0:T(8,128)S(1)}, f32[53,7,128]{2,1,0:T(8,128)S(1)}, u32[]{:S(2)}, u32[]{:S(2)}) collective-permute-start(f32[53,7,128]{2,1,0:T(8,128)S(1)} %get-tuple-element.287), channel_id=1, source_target_pairs={{8,0},{16,8},{24,16},{9,1},{17,9},{25,17},{10,2},{18,10},{26,18},{... | collective-permute-start | bytes 569864 | tf_op jit(solution)/shard_map/ppermute | solution.py:162
  11.7 5.7 %copy-start.1 = (f32[16,16,128]{2,1,0:T(8,128)S(1)}, f32[16,16,128]{2,1,0:T(8,128)}, u32[]{:S(2)}) copy-start(f32[16,16,128]{2,1,0:T(8,128)} %param.9) | copy-start | bytes 393220
  14.3 3.2 %copy-start.2 = (f32[2,16,128]{2,1,0:T(8,128)S(1)}, f32[2,16,128]{2,1,0:T(8,128)}, u32[]{:S(2)}) copy-start(f32[2,16,128]{2,1,0:T(8,128)} %param.10) | copy-start | bytes 49156
  14.3 3.2 %copy-start.5 = (s32[16,128]{1,0:T(8,128)S(1)}, s32[16,128]{1,0:T(8,128)}, u32[]{:S(2)}) copy-start(s32[16,128]{1,0:T(8,128)} %param.12) | copy-start | bytes 24580
  15.4 2.8 %copy-start.6 = (s32[16,128]{1,0:T(8,128)S(1)}, s32[16,128]{1,0:T(8,128)}, u32[]{:S(2)}) copy-start(s32[16,128]{1,0:T(8,128)} %param.13) | copy-start | bytes 24580
  15.4 3.6 %copy-start.7 = (f32[1,16]{1,0:T(1,128)S(1)}, f32[1,16]{1,0:T(1,128)}, u32[]{:S(2)}) copy-start(f32[1,16]{1,0:T(1,128)} %param.11) | copy-start | bytes 196
  19.0 8.6 %collective-permute-start.5 = (f32[3,16]{1,0:T(4,128)S(1)}, f32[3,16]{1,0:T(4,128)S(1)}, u32[]{:S(2)}, u32[]{:S(2)}) collective-permute-start(f32[3,16]{1,0:T(4,128)S(1)} %pad_maximum_fusion.17), channel_id=1, source_target_pairs={{0,7},{1,0},{2,1},{3,2},{4,3},{5,4},{6,5},{7,6},{8,15},{9,8},{10,9... | collective-permute-start | bytes 584 | tf_op jit(solution)/shard_map/ppermute | solution.py:215
  19.9 5.8 %collective-permute-start.4 = (f32[3,16]{1,0:T(4,128)S(1)}, f32[3,16]{1,0:T(4,128)S(1)}, u32[]{:S(2)}, u32[]{:S(2)}) collective-permute-start(f32[3,16]{1,0:T(4,128)S(1)} %pad_maximum_fusion.17), channel_id=1, source_target_pairs={{0,1},{1,2},{2,3},{3,4},{4,5},{5,6},{6,7},{7,0},{8,9},{9,10},{10,1... | collective-permute-start | bytes 584 | tf_op jit(solution)/shard_map/ppermute | solution.py:210
  20.9 17.8 %collective-permute-start.3 = (f32[52,30,7]{0,1,2:T(8,128)S(1)}, f32[52,30,7]{0,1,2:T(8,128)S(1)}, u32[]{:S(2)}, u32[]{:S(2)}) collective-permute-start(f32[52,30,7]{0,1,2:T(8,128)S(1)} %pad_maximum_fusion.6), channel_id=1, source_target_pairs={{1,0},{2,1},{3,2},{4,3},{5,4},{6,5},{7,6},{9,8},{10,9},{11,10},{12... | collective-permute-start | bytes 131048 | tf_op jit(solution)/shard_map/ppermute | solution.py:162
  22.2 15.6 %collective-permute-start.2 = (f32[52,30,7]{0,1,2:T(8,128)S(1)}, f32[52,30,7]{0,1,2:T(8,128)S(1)}, u32[]{:S(2)}, u32[]{:S(2)}) collective-permute-start(f32[52,30,7]{0,1,2:T(8,128)S(1)} %pad_maximum_fusion.5), channel_id=1, source_target_pairs={{0,1},{1,2},{2,3},{3,4},{4,5},{5,6},{6,7},{8,9},{9,10},{10,11},{11... | collective-permute-start | bytes 131048 | tf_op jit(solution)/shard_map/ppermute | solution.py:162
  25.8 4.0 %collective-permute-start.6 = (f32[3,16]{1,0:T(4,128)S(1)}, f32[3,16]{1,0:T(4,128)S(1)}, u32[]{:S(2)}, u32[]{:S(2)}) collective-permute-start(f32[3,16]{1,0:T(4,128)S(1)} %collective-permute-done.4), channel_id=1, source_target_pairs={{0,1},{1,2},{2,3},{3,4},{4,5},{5,6},{6,7},{7,0},{8,9},{9,10},{10,1... | collective-permute-start | bytes 584 | tf_op jit(solution)/shard_map/ppermute | solution.py:210
  27.7 2.1 %collective-permute-start.7 = (f32[3,16]{1,0:T(4,128)S(1)}, f32[3,16]{1,0:T(4,128)S(1)}, u32[]{:S(2)}, u32[]{:S(2)}) collective-permute-start(f32[3,16]{1,0:T(4,128)S(1)} %collective-permute-done.5), channel_id=1, source_target_pairs={{0,7},{1,0},{2,1},{3,2},{4,3},{5,4},{6,5},{7,6},{8,15},{9,8},{10,9... | collective-permute-start | bytes 584 | tf_op jit(solution)/shard_map/ppermute | solution.py:215
  29.7 3.9 %collective-permute-start.8 = (f32[3,16]{1,0:T(4,128)S(1)}, f32[3,16]{1,0:T(4,128)S(1)}, u32[]{:S(2)}, u32[]{:S(2)}) collective-permute-start(f32[3,16]{1,0:T(4,128)S(1)} %collective-permute-done.6), channel_id=1, source_target_pairs={{0,1},{1,2},{2,3},{3,4},{4,5},{5,6},{6,7},{7,0},{8,9},{9,10},{10,1... | collective-permute-start | bytes 584 | tf_op jit(solution)/shard_map/ppermute | solution.py:210
  29.8 4.1 %collective-permute-start.9 = (f32[3,16]{1,0:T(4,128)S(1)}, f32[3,16]{1,0:T(4,128)S(1)}, u32[]{:S(2)}, u32[]{:S(2)}) collective-permute-start(f32[3,16]{1,0:T(4,128)S(1)} %collective-permute-done.7), channel_id=1, source_target_pairs={{0,7},{1,0},{2,1},{3,2},{4,3},{5,4},{6,5},{7,6},{8,15},{9,8},{10,9... | collective-permute-start | bytes 584 | tf_op jit(solution)/shard_map/ppermute | solution.py:215
  33.6 3.9 %collective-permute-start.10 = (f32[3,16]{1,0:T(4,128)S(1)}, f32[3,16]{1,0:T(4,128)S(1)}, u32[]{:S(2)}, u32[]{:S(2)}) collective-permute-start(f32[3,16]{1,0:T(4,128)S(1)} %collective-permute-done.8), channel_id=1, source_target_pairs={{0,1},{1,2},{2,3},{3,4},{4,5},{5,6},{6,7},{7,0},{8,9},{9,10},{10,1... | collective-permute-start | bytes 584 | tf_op jit(solution)/shard_map/ppermute | solution.py:210
  40.7 3.0 %copy-start.3 = (f32[284]{0:T(512)S(1)}, f32[284]{0:T(512)}, u32[]{:S(2)}) copy-start(f32[284]{0:T(512)} %constant.96.clone.1) | copy-start | bytes 3412
  40.7 3.0 %copy-start.4 = (f32[284]{0:T(512)S(1)}, f32[284]{0:T(512)}, u32[]{:S(2)}) copy-start(f32[284]{0:T(512)} %constant.94.clone.1) | copy-start | bytes 3412
